TPU v7x, 32 devices: a whole 2x2x4 slice. The times are simulated.
32 devices in a mesh: gx: 4 (over y, x), gy: 8 (over z, core).
Axes of the slice: x: 2, y: 2, z: 4, core: 2. Of those that a mesh axis runs over, the one named last changes fastest.
Arguments:
- start_field: float32 [64, 64, 512], P('gx', 'gy'), may hold values from -6 to 6
- right_side: float32 [64, 64, 512], P('gx', 'gy'), may hold values from -12 to 12
- accumulation: float32 [64, 64, 512], P('gx', 'gy'), may hold values from 0.05 to 1
- trans_x: float32 [64, 64, 512], P('gx', 'gy'), may hold values from 0.1 to 10
- trans_y: float32 [64, 64, 512], P('gx', 'gy'), may hold values from 0.1 to 10
- trans_z: float32 [64, 64, 512], P('gx', 'gy'), may hold values from 0.1 to 10
Outputs:
- ortho_basis: float32 [5, 64, 64, 512], P(None, 'gx', 'gy')
- upper_factor: float32 [5, 5], replicated
- residual_scale: float32 [], replicated
All inputs are finite; a program needn't handle non-finite values.
Results may differ from a plain program's by a relative error of at most 0.0003.
Values sent between devices are 32-bit elements; how exact they have to be, the bound alone decides.
No kernel may reach another device: no remote copies, remote signals or barrier semaphores. Data moves between devices by JAX's collectives and lax.ppermute only.
A program may use at most 64 MiB of HBM per device.

v0:
```python
import jax
import jax.numpy as jnp
from jax import lax
from jax.sharding import PartitionSpec as P

STEPS = 4
EPS = 1e-06


def padded(block, sides, width):
    for axis, dim in sides:
        count = lax.axis_size(axis)
        forward = [(i, i + 1) for i in range(count - 1)]
        backward = [(target, source) for source, target in forward]
        low = lax.ppermute(
            lax.slice_in_dim(block, block.shape[dim] - width, None, axis=dim), axis, forward
        )
        high = lax.ppermute(lax.slice_in_dim(block, 0, width, axis=dim), axis, backward)
        block = jnp.concatenate([low, block, high], axis=dim)
    return block


def from_behind(value, axis, by):
    peers = lax.axis_size(axis)
    pairs = [(i, i + by) for i in range(peers) if 0 <= i + by < peers]
    return lax.ppermute(value, axis, pairs)


def neighbours(field, coef):
    acc_c, t_x, t_y, t_z = coef
    lx = field.shape[0] - 2
    ly = field.shape[1] - 2
    ox = (t_x.shape[0] - lx) // 2
    oy = (t_x.shape[1] - ly) // 2

    def piece(a, dx, dy):
        return a[ox + dx : ox + dx + lx, oy + dy : oy + dy + ly]

    centre = field[1:-1, 1:-1]
    zero_plane = jnp.zeros_like(centre[..., :1])
    tz_low = piece(t_z, 0, 0)
    tz_high = jnp.concatenate([tz_low[..., 1:], zero_plane], axis=-1)
    z_low = jnp.concatenate([zero_plane, centre[..., :-1]], axis=-1)
    z_high = jnp.concatenate([centre[..., 1:], zero_plane], axis=-1)
    tx_low = piece(t_x, 0, 0)
    tx_high = piece(t_x, 1, 0)
    ty_low = piece(t_y, 0, 0)
    ty_high = piece(t_y, 0, 1)
    total = tx_low * field[:-2, 1:-1] + tx_high * field[2:, 1:-1]
    total = total + ty_low * field[1:-1, :-2] + ty_high * field[1:-1, 2:]
    total = total + tz_low * z_low + tz_high * z_high
    diagonal = piece(acc_c, 0, 0) + tx_low + tx_high + ty_low + ty_high + tz_low + tz_high
    return (total, diagonal)


def upper_inverse(upper):
    size = upper.shape[0]
    columns = []
    for col in range(size):
        values = [None] * size
        for row in reversed(range(size)):
            value = jnp.float32(1.0 if row == col else 0.0)
            for inner in range(row + 1, size):
                value = value - upper[row, inner] * values[inner]
            values[row] = value / upper[row, row]
        columns.append(jnp.stack(values))
    return jnp.stack(columns, axis=1)


def pad_plain(a):
    return jnp.pad(a, ((1, 1), (1, 1), (0, 0)))


def field_widen(field):
    return padded(field, (("gx", 0), ("gy", 1)), 1)


def local(start_field, right_side, accumulation, trans_x, trans_y, trans_z):
    size_x, size_y, size_z = start_field.shape
    cells = size_x * size_y * size_z * lax.axis_size("gx") * lax.axis_size("gy")
    plane_x = from_behind(trans_x[:1], "gx", -1)
    plane_y = from_behind(trans_y[:, :1], "gy", -1)
    rim_x = jnp.pad(jnp.concatenate([trans_x, plane_x], axis=0), ((1, 0), (1, 1), (0, 0)))
    rim_y = jnp.pad(jnp.concatenate([trans_y, plane_y], axis=1), ((1, 1), (1, 0), (0, 0)))
    coef = (pad_plain(accumulation), rim_x, rim_y, pad_plain(trans_z))
    total, diagonal = neighbours(field_widen(start_field), coef)
    residual0 = right_side - (diagonal * start_field - total)
    squares = lax.psum(jnp.sum(residual0 * residual0), ("gx", "gy"))
    scale = jnp.sqrt(squares / cells + EPS)
    vector = residual0 / scale
    basis = [residual0 / scale]
    for step in range(STEPS):
        total, diagonal = neighbours(field_widen(vector), coef)
        vector = 2.0 * total / diagonal
        basis.append(vector)
    block = jnp.stack(basis)
    local_gram = jnp.einsum("axyz,bxyz->ab", block, block, precision=lax.Precision.HIGHEST)
    gram = lax.psum(local_gram, ("gx", "gy")) / cells
    upper = jnp.linalg.cholesky(gram).T
    inverse = upper_inverse(upper)
    ortho = jnp.einsum("jk,jxyz->kxyz", inverse, block, precision=lax.Precision.HIGHEST)
    return (ortho, upper, scale)


def solution(mesh):
    in_specs = (
        P("gx", "gy", None),
        P("gx", "gy", None),
        P("gx", "gy", None),
        P("gx", "gy", None),
        P("gx", "gy", None),
        P("gx", "gy", None),
    )
    out_specs = (P(None, "gx", "gy", None), P(), P())
    return jax.shard_map(local, mesh=mesh, in_specs=in_specs, out_specs=out_specs, check_vma=False)
```

profile of v0, /device:TPU:0, one launch (start us, length us, event | category | flops | bytes accessed | tf_op | source)
XLA Modules:
  0.0 220.1 jit_solution(5682292001169341076)
XLA Ops:
  0.7 0.8 fusion.73
  1.5 4.8 %collective-permute-start.2 = (f32[1,8,512]{2,1,0:T(8,128)S(1)}, f32[1,8,512]{2,1,0:T(8,128)S(1)}, u32[]{:S(2)}, u32[]{:S(2)}) collective-permute-start(f32[1,8,512]{2,1,0:T(8,128)S(1)} %get-tuple-element.35), channel_id=1, source_target_pairs={{0,8},{8,16},{16,24},{1,9},{9,17},{17,25},{2,10},{10,18},{18,26},{... | collective-permute-start | bytes 49160 | tf_op jit(solution)/shard_map/ppermute | solution.py:15
  6.4 0.7 slice.332
  7.1 1.3 collective-permute-start
  8.4 1.3 collective-permute-start.3
  9.7 1.0 slice.334
  10.7 1.3 collective-permute-start.1
  12.0 1.0 constant_dynamic-update-slice_fusion.1
  13.0 1.7 collective-permute-done.3
  14.7 1.4 collective-permute-start.4
  16.1 1.3 collective-permute-start.5
  17.4 1.2 fusion.74
  18.6 0.1 slice.336
  18.7 2.2 %collective-permute-done.5 = f32[18,1,512]{2,1,0:T(1,128)S(1)} collective-permute-done((f32[18,1,512]{2,1,0:T(1,128)S(1)}, f32[18,1,512]{2,1,0:T(1,128)S(1)}, u32[]{:S(2)}, u32[]{:S(2)}) %collective-permute-start.5) | collective-permute-done | bytes 36896 | tf_op jit(solution)/shard_map/ppermute | solution.py:18
  21.0 1.0 multiply_reduce_fusion
  21.9 44.0 %psum.14 = f32[]{:T(128)} all-reduce(f32[]{:T(128)} %get-tuple-element.6), channel_id=1, replica_groups=mesh['gx'=4,'gy'=8] {'gx','gy'}, use_global_device_ids=true, to_apply=%region_1.2 | all-reduce | flops 1 | bytes 8 | tf_op jit(solution)/shard_map/psum | solution.py:88
  66.7 4.2 %collective-permute-start.6 = (f32[1,8,512]{2,1,0:T(8,128)S(1)}, f32[1,8,512]{2,1,0:T(8,128)S(1)}, u32[]{:S(2)}, u32[]{:S(2)}) collective-permute-start(f32[1,8,512]{2,1,0:T(8,128)S(1)} %get-tuple-element.32), channel_id=1, source_target_pairs={{0,8},{8,16},{16,24},{1,9},{9,17},{17,25},{2,10},{10,18},{18,26},{... | collective-permute-start | bytes 49160 | tf_op jit(solution)/shard_map/ppermute | solution.py:15
  70.9 1.3 collective-permute-start.7
  72.2 0.1 collective-permute-done.6
  72.3 4.2 %collective-permute-done.7 = f32[1,8,512]{2,1,0:T(8,128)S(1)} collective-permute-done((f32[1,8,512]{2,1,0:T(8,128)S(1)}, f32[1,8,512]{2,1,0:T(8,128)S(1)}, u32[]{:S(2)}, u32[]{:S(2)}) %collective-permute-start.7) | collective-permute-done | bytes 16416 | tf_op jit(solution)/shard_map/ppermute | solution.py:18
  76.6 1.3 collective-permute-start.8
  77.9 1.3 collective-permute-start.9
  79.2 0.1 fusion.71
  79.3 3.2 %collective-permute-done.9 = f32[18,1,512]{2,1,0:T(1,128)S(1)} collective-permute-done((f32[18,1,512]{2,1,0:T(1,128)S(1)}, f32[18,1,512]{2,1,0:T(1,128)S(1)}, u32[]{:S(2)}, u32[]{:S(2)}) %collective-permute-start.9) | collective-permute-done | bytes 36896 | tf_op jit(solution)/shard_map/ppermute | solution.py:18
  82.6 0.3 fusion.38
  82.9 4.5 %collective-permute-start.10 = (f32[1,8,512]{2,1,0:T(8,128)S(1)}, f32[1,8,512]{2,1,0:T(8,128)S(1)}, u32[]{:S(2)}, u32[]{:S(2)}) collective-permute-start(f32[1,8,512]{2,1,0:T(8,128)S(1)} %get-tuple-element.28), channel_id=1, source_target_pairs={{0,8},{8,16},{16,24},{1,9},{9,17},{17,25},{2,10},{10,18},{18,26},{... | collective-permute-start | bytes 49160 | tf_op jit(solution)/shard_map/ppermute | solution.py:15
  87.4 1.3 collective-permute-start.11
  88.8 4.2 %collective-permute-done.11 = f32[1,8,512]{2,1,0:T(8,128)S(1)} collective-permute-done((f32[1,8,512]{2,1,0:T(8,128)S(1)}, f32[1,8,512]{2,1,0:T(8,128)S(1)}, u32[]{:S(2)}, u32[]{:S(2)}) %collective-permute-start.11) | collective-permute-done | bytes 16416 | tf_op jit(solution)/shard_map/ppermute | solution.py:18
  93.1 3.1 %collective-permute-start.12 = (f32[18,1,512]{2,1,0:T(1,128)S(1)}, f32[18,1,512]{2,1,0:T(1,128)S(1)}, u32[]{:S(2)}, u32[]{:S(2)}) collective-permute-start(f32[18,1,512]{2,1,0:T(1,128)S(1)} %get-tuple-element.12), channel_id=1, source_target_pairs={{0,1},{1,2},{2,3},{3,4},{4,5},{5,6},{6,7},{8,9},{9,10},{10,11},{11... | collective-permute-start | bytes 110600 | tf_op jit(solution)/shard_map/ppermute | solution.py:15
  96.2 1.3 collective-permute-start.13
  97.5 0.1 fusion.69
  97.7 2.6 %collective-permute-done.13 = f32[18,1,512]{2,1,0:T(1,128)S(1)} collective-permute-done((f32[18,1,512]{2,1,0:T(1,128)S(1)}, f32[18,1,512]{2,1,0:T(1,128)S(1)}, u32[]{:S(2)}, u32[]{:S(2)}) %collective-permute-start.13) | collective-permute-done | bytes 36896 | tf_op jit(solution)/shard_map/ppermute | solution.py:18
  100.3 0.3 fusion.27
  100.6 2.8 %collective-permute-start.14 = (f32[1,8,512]{2,1,0:T(8,128)S(1)}, f32[1,8,512]{2,1,0:T(8,128)S(1)}, u32[]{:S(2)}, u32[]{:S(2)}) collective-permute-start(f32[1,8,512]{2,1,0:T(8,128)S(1)} %get-tuple-element.24), channel_id=1, source_target_pairs={{0,8},{8,16},{16,24},{1,9},{9,17},{17,25},{2,10},{10,18},{18,26},{... | collective-permute-start | bytes 49160 | tf_op jit(solution)/shard_map/ppermute | solution.py:15
  103.5 1.3 collective-permute-start.15
  104.9 4.2 %collective-permute-done.15 = f32[1,8,512]{2,1,0:T(8,128)S(1)} collective-permute-done((f32[1,8,512]{2,1,0:T(8,128)S(1)}, f32[1,8,512]{2,1,0:T(8,128)S(1)}, u32[]{:S(2)}, u32[]{:S(2)}) %collective-permute-start.15) | collective-permute-done | bytes 16416 | tf_op jit(solution)/shard_map/ppermute | solution.py:18
  109.1 3.1 %collective-permute-start.16 = (f32[18,1,512]{2,1,0:T(1,128)S(1)}, f32[18,1,512]{2,1,0:T(1,128)S(1)}, u32[]{:S(2)}, u32[]{:S(2)}) collective-permute-start(f32[18,1,512]{2,1,0:T(1,128)S(1)} %get-tuple-element.10), channel_id=1, source_target_pairs={{0,1},{1,2},{2,3},{3,4},{4,5},{5,6},{6,7},{8,9},{9,10},{10,11},{11... | collective-permute-start | bytes 110600 | tf_op jit(solution)/shard_map/ppermute | solution.py:15
  112.3 1.3 collective-permute-start.17
  113.6 0.1 fusion.67
  113.7 2.6 %collective-permute-done.17 = f32[18,1,512]{2,1,0:T(1,128)S(1)} collective-permute-done((f32[18,1,512]{2,1,0:T(1,128)S(1)}, f32[18,1,512]{2,1,0:T(1,128)S(1)}, u32[]{:S(2)}, u32[]{:S(2)}) %collective-permute-start.17) | collective-permute-done | bytes 36896 | tf_op jit(solution)/shard_map/ppermute | solution.py:18
  116.3 0.3 fusion.16
  116.7 2.8 %collective-permute-start.18 = (f32[1,8,512]{2,1,0:T(8,128)S(1)}, f32[1,8,512]{2,1,0:T(8,128)S(1)}, u32[]{:S(2)}, u32[]{:S(2)}) collective-permute-start(f32[1,8,512]{2,1,0:T(8,128)S(1)} %get-tuple-element.20), channel_id=1, source_target_pairs={{0,8},{8,16},{16,24},{1,9},{9,17},{17,25},{2,10},{10,18},{18,26},{... | collective-permute-start | bytes 49160 | tf_op jit(solution)/shard_map/ppermute | solution.py:15
  119.5 1.3 collective-permute-start.19
  120.9 0.3 copy.9
  121.1 0.3 copy.10
  121.4 0.3 copy.11
  121.7 3.5 %collective-permute-done.19 = f32[1,8,512]{2,1,0:T(8,128)S(1)} collective-permute-done((f32[1,8,512]{2,1,0:T(8,128)S(1)}, f32[1,8,512]{2,1,0:T(8,128)S(1)}, u32[]{:S(2)}, u32[]{:S(2)}) %collective-permute-start.19) | collective-permute-done | bytes 16416 | tf_op jit(solution)/shard_map/ppermute | solution.py:18
  125.2 3.1 %collective-permute-start.20 = (f32[18,1,512]{2,1,0:T(1,128)S(1)}, f32[18,1,512]{2,1,0:T(1,128)S(1)}, u32[]{:S(2)}, u32[]{:S(2)}) collective-permute-start(f32[18,1,512]{2,1,0:T(1,128)S(1)} %get-tuple-element.8), channel_id=1, source_target_pairs={{0,1},{1,2},{2,3},{3,4},{4,5},{5,6},{6,7},{8,9},{9,10},{10,11},{11... | collective-permute-start | bytes 110600 | tf_op jit(solution)/shard_map/ppermute | solution.py:15
  128.4 1.3 collective-permute-start.21
  129.7 0.1 fusion.65
  129.8 0.3 copy.12
  130.1 2.3 %collective-permute-done.21 = f32[18,1,512]{2,1,0:T(1,128)S(1)} collective-permute-done((f32[18,1,512]{2,1,0:T(1,128)S(1)}, f32[18,1,512]{2,1,0:T(1,128)S(1)}, u32[]{:S(2)}, u32[]{:S(2)}) %collective-permute-start.21) | collective-permute-done | bytes 36896 | tf_op jit(solution)/shard_map/ppermute | solution.py:18
  132.4 0.4 fusion.5
  132.8 0.2 stack.118
  132.9 2.1 stack.119
  135.0 4.6 %convolution_bitcast_fusion = f32[5,5]{0,1:T(8,128)S(1)} fusion(f32[5,16,8,512]{3,0,2,1:T(8,128)S(1)} %stack.119), kind=kOutput, calls=%fused_computation | convolution fusion | flops 19660800 | bytes 1310820 | tf_op jit(solution)/shard_map/axyz,bxyz->ab/dot_general | solution.py:97
  139.6 40.9 %psum.15 = f32[5,5]{0,1:T(8,128)S(1)} all-reduce(f32[5,5]{0,1:T(8,128)S(1)} %convolution_bitcast_fusion), channel_id=1, replica_groups=mesh['gx'=4,'gy'=8] {'gx','gy'}, use_global_device_ids=true, to_apply=%region_2.3 | all-reduce | flops 25 | bytes 200 | tf_op jit(solution)/shard_map/psum | solution.py:98
  180.6 0.4 cholesky.18
  181.0 0.6 compare_reduce_fusion
  181.7 0.6 select_bitcast_fusion
  182.4 0.7 copy.16
  183.0 0.7 fusion.75
  215.3 1.8 fusion.60
  217.1 1.8 copy.15
  (46 shorter events, 1.2 us)
Async XLA Ops:
  0.6 20.3 %copy-start.4 = (f32[16,8,512]{2,1,0:T(8,128)S(1)}, f32[16,8,512]{2,1,0:T(8,128)}, u32[]{:S(2)}) copy-start(f32[16,8,512]{2,1,0:T(8,128)} %param.6) | copy-start | bytes 786436
  0.6 20.3 %copy-start.2 = (f32[16,8,512]{2,1,0:T(8,128)S(1)}, f32[16,8,512]{2,1,0:T(8,128)}, u32[]{:S(2)}) copy-start(f32[16,8,512]{2,1,0:T(8,128)} %param.9) | copy-start | bytes 786436
  0.7 20.3 %copy-start.1 = (f32[16,8,512]{2,1,0:T(8,128)S(1)}, f32[16,8,512]{2,1,0:T(8,128)}, u32[]{:S(2)}) copy-start(f32[16,8,512]{2,1,0:T(8,128)} %param.10) | copy-start | bytes 786436
  0.7 17.9 %copy-start = (f32[16,8,512]{2,1,0:T(8,128)S(1)}, f32[16,8,512]{2,1,0:T(8,128)}, u32[]{:S(2)}) copy-start(f32[16,8,512]{2,1,0:T(8,128)} %param.11) | copy-start | bytes 786436
  0.7 20.3 %copy-start.3 = (f32[16,8,512]{2,1,0:T(8,128)S(1)}, f32[16,8,512]{2,1,0:T(8,128)}, u32[]{:S(2)}) copy-start(f32[16,8,512]{2,1,0:T(8,128)} %param.8) | copy-start | bytes 786436
  0.7 20.3 %copy-start.5 = (f32[16,8,512]{2,1,0:T(8,128)S(1)}, f32[16,8,512]{2,1,0:T(8,128)}, u32[]{:S(2)}) copy-start(f32[16,8,512]{2,1,0:T(8,128)} %param.7) | copy-start | bytes 786436
  1.5 10.4 %collective-permute-start.2 = (f32[1,8,512]{2,1,0:T(8,128)S(1)}, f32[1,8,512]{2,1,0:T(8,128)S(1)}, u32[]{:S(2)}, u32[]{:S(2)}) collective-permute-start(f32[1,8,512]{2,1,0:T(8,128)S(1)} %get-tuple-element.35), channel_id=1, source_target_pairs={{0,8},{8,16},{16,24},{1,9},{9,17},{17,25},{2,10},{10,18},{18,26},{... | collective-permute-start | bytes 49160 | tf_op jit(solution)/shard_map/ppermute | solution.py:15
  7.1 11.6 %collective-permute-start = (f32[1,8,512]{2,1,0:T(8,128)S(1)}, f32[1,8,512]{2,1,0:T(8,128)S(1)}, u32[]{:S(2)}, u32[]{:S(2)}) collective-permute-start(f32[1,8,512]{2,1,0:T(8,128)S(1)} %slice.332), channel_id=1, source_target_pairs={{8,0},{16,8},{24,16},{9,1},{17,9},{25,17},{10,2},{18,10},{26,18},{... | collective-permute-start | bytes 49160 | tf_op jit(solution)/shard_map/ppermute | solution.py:26
  8.4 6.3 %collective-permute-start.3 = (f32[1,8,512]{2,1,0:T(8,128)S(1)}, f32[1,8,512]{2,1,0:T(8,128)S(1)}, u32[]{:S(2)}, u32[]{:S(2)}) collective-permute-start(f32[1,8,512]{2,1,0:T(8,128)S(1)} %get-tuple-element.34), channel_id=1, source_target_pairs={{8,0},{16,8},{24,16},{9,1},{17,9},{25,17},{10,2},{18,10},{26,18},{... | collective-permute-start | bytes 49160 | tf_op jit(solution)/shard_map/ppermute | solution.py:18
  10.7 8.0 %collective-permute-start.1 = (f32[16,1,512]{2,1,0:T(1,128)S(1)}, f32[16,1,512]{2,1,0:T(1,128)S(1)}, u32[]{:S(2)}, u32[]{:S(2)}) collective-permute-start(f32[16,1,512]{2,1,0:T(1,128)S(1)} %slice.334), channel_id=1, source_target_pairs={{1,0},{2,1},{3,2},{4,3},{5,4},{6,5},{7,6},{9,8},{10,9},{11,10},{12... | collective-permute-start | bytes 98312 | tf_op jit(solution)/shard_map/ppermute | solution.py:26
  14.7 4.0 %collective-permute-start.4 = (f32[18,1,512]{2,1,0:T(1,128)S(1)}, f32[18,1,512]{2,1,0:T(1,128)S(1)}, u32[]{:S(2)}, u32[]{:S(2)}) collective-permute-start(f32[18,1,512]{2,1,0:T(1,128)S(1)} %get-tuple-element.16), channel_id=1, source_target_pairs={{0,1},{1,2},{2,3},{3,4},{4,5},{5,6},{6,7},{8,9},{9,10},{10,11},{11... | collective-permute-start | bytes 110600 | tf_op jit(solution)/shard_map/ppermute | solution.py:15
  16.1 4.8 %collective-permute-start.5 = (f32[18,1,512]{2,1,0:T(1,128)S(1)}, f32[18,1,512]{2,1,0:T(1,128)S(1)}, u32[]{:S(2)}, u32[]{:S(2)}) collective-permute-start(f32[18,1,512]{2,1,0:T(1,128)S(1)} %get-tuple-element.17), channel_id=1, source_target_pairs={{1,0},{2,1},{3,2},{4,3},{5,4},{6,5},{7,6},{9,8},{10,9},{11,10},{12... | collective-permute-start | bytes 110600 | tf_op jit(solution)/shard_map/ppermute | solution.py:18
  66.7 5.6 %collective-permute-start.6 = (f32[1,8,512]{2,1,0:T(8,128)S(1)}, f32[1,8,512]{2,1,0:T(8,128)S(1)}, u32[]{:S(2)}, u32[]{:S(2)}) collective-permute-start(f32[1,8,512]{2,1,0:T(8,128)S(1)} %get-tuple-element.32), channel_id=1, source_target_pairs={{0,8},{8,16},{16,24},{1,9},{9,17},{17,25},{2,10},{10,18},{18,26},{... | collective-permute-start | bytes 49160 | tf_op jit(solution)/shard_map/ppermute | solution.py:15
  70.9 5.6 %collective-permute-start.7 = (f32[1,8,512]{2,1,0:T(8,128)S(1)}, f32[1,8,512]{2,1,0:T(8,128)S(1)}, u32[]{:S(2)}, u32[]{:S(2)}) collective-permute-start(f32[1,8,512]{2,1,0:T(8,128)S(1)} %get-tuple-element.33), channel_id=1, source_target_pairs={{8,0},{16,8},{24,16},{9,1},{17,9},{25,17},{10,2},{18,10},{26,18},{... | collective-permute-start | bytes 49160 | tf_op jit(solution)/shard_map/ppermute | solution.py:18
  76.6 2.7 %collective-permute-start.8 = (f32[18,1,512]{2,1,0:T(1,128)S(1)}, f32[18,1,512]{2,1,0:T(1,128)S(1)}, u32[]{:S(2)}, u32[]{:S(2)}) collective-permute-start(f32[18,1,512]{2,1,0:T(1,128)S(1)} %get-tuple-element.14), channel_id=1, source_target_pairs={{0,1},{1,2},{2,3},{3,4},{4,5},{5,6},{6,7},{8,9},{9,10},{10,11},{11... | collective-permute-start | bytes 110600 | tf_op jit(solution)/shard_map/ppermute | solution.py:15
  77.9 4.7 %collective-permute-start.9 = (f32[18,1,512]{2,1,0:T(1,128)S(1)}, f32[18,1,512]{2,1,0:T(1,128)S(1)}, u32[]{:S(2)}, u32[]{:S(2)}) collective-permute-start(f32[18,1,512]{2,1,0:T(1,128)S(1)} %get-tuple-element.15), channel_id=1, source_target_pairs={{1,0},{2,1},{3,2},{4,3},{5,4},{6,5},{7,6},{9,8},{10,9},{11,10},{12... | collective-permute-start | bytes 110600 | tf_op jit(solution)/shard_map/ppermute | solution.py:18
  82.9 5.9 %collective-permute-start.10 = (f32[1,8,512]{2,1,0:T(8,128)S(1)}, f32[1,8,512]{2,1,0:T(8,128)S(1)}, u32[]{:S(2)}, u32[]{:S(2)}) collective-permute-start(f32[1,8,512]{2,1,0:T(8,128)S(1)} %get-tuple-element.28), channel_id=1, source_target_pairs={{0,8},{8,16},{16,24},{1,9},{9,17},{17,25},{2,10},{10,18},{18,26},{... | collective-permute-start | bytes 49160 | tf_op jit(solution)/shard_map/ppermute | solution.py:15
  87.4 5.6 %collective-permute-start.11 = (f32[1,8,512]{2,1,0:T(8,128)S(1)}, f32[1,8,512]{2,1,0:T(8,128)S(1)}, u32[]{:S(2)}, u32[]{:S(2)}) collective-permute-start(f32[1,8,512]{2,1,0:T(8,128)S(1)} %get-tuple-element.29), channel_id=1, source_target_pairs={{8,0},{16,8},{24,16},{9,1},{17,9},{25,17},{10,2},{18,10},{26,18},{... | collective-permute-start | bytes 49160 | tf_op jit(solution)/shard_map/ppermute | solution.py:18
  93.1 4.6 %collective-permute-start.12 = (f32[18,1,512]{2,1,0:T(1,128)S(1)}, f32[18,1,512]{2,1,0:T(1,128)S(1)}, u32[]{:S(2)}, u32[]{:S(2)}) collective-permute-start(f32[18,1,512]{2,1,0:T(1,128)S(1)} %get-tuple-element.12), channel_id=1, source_target_pairs={{0,1},{1,2},{2,3},{3,4},{4,5},{5,6},{6,7},{8,9},{9,10},{10,11},{11... | collective-permute-start | bytes 110600 | tf_op jit(solution)/shard_map/ppermute | solution.py:15
  96.2 4.0 %collective-permute-start.13 = (f32[18,1,512]{2,1,0:T(1,128)S(1)}, f32[18,1,512]{2,1,0:T(1,128)S(1)}, u32[]{:S(2)}, u32[]{:S(2)}) collective-permute-start(f32[18,1,512]{2,1,0:T(1,128)S(1)} %get-tuple-element.13), channel_id=1, source_target_pairs={{1,0},{2,1},{3,2},{4,3},{5,4},{6,5},{7,6},{9,8},{10,9},{11,10},{12... | collective-permute-start | bytes 110600 | tf_op jit(solution)/shard_map/ppermute | solution.py:18
  100.6 4.3 %collective-permute-start.14 = (f32[1,8,512]{2,1,0:T(8,128)S(1)}, f32[1,8,512]{2,1,0:T(8,128)S(1)}, u32[]{:S(2)}, u32[]{:S(2)}) collective-permute-start(f32[1,8,512]{2,1,0:T(8,128)S(1)} %get-tuple-element.24), channel_id=1, source_target_pairs={{0,8},{8,16},{16,24},{1,9},{9,17},{17,25},{2,10},{10,18},{18,26},{... | collective-permute-start | bytes 49160 | tf_op jit(solution)/shard_map/ppermute | solution.py:15
  103.5 5.6 %collective-permute-start.15 = (f32[1,8,512]{2,1,0:T(8,128)S(1)}, f32[1,8,512]{2,1,0:T(8,128)S(1)}, u32[]{:S(2)}, u32[]{:S(2)}) collective-permute-start(f32[1,8,512]{2,1,0:T(8,128)S(1)} %get-tuple-element.25), channel_id=1, source_target_pairs={{8,0},{16,8},{24,16},{9,1},{17,9},{25,17},{10,2},{18,10},{26,18},{... | collective-permute-start | bytes 49160 | tf_op jit(solution)/shard_map/ppermute | solution.py:18
  109.1 4.6 %collective-permute-start.16 = (f32[18,1,512]{2,1,0:T(1,128)S(1)}, f32[18,1,512]{2,1,0:T(1,128)S(1)}, u32[]{:S(2)}, u32[]{:S(2)}) collective-permute-start(f32[18,1,512]{2,1,0:T(1,128)S(1)} %get-tuple-element.10), channel_id=1, source_target_pairs={{0,1},{1,2},{2,3},{3,4},{4,5},{5,6},{6,7},{8,9},{9,10},{10,11},{11... | collective-permute-start | bytes 110600 | tf_op jit(solution)/shard_map/ppermute | solution.py:15
  112.3 4.0 %collective-permute-start.17 = (f32[18,1,512]{2,1,0:T(1,128)S(1)}, f32[18,1,512]{2,1,0:T(1,128)S(1)}, u32[]{:S(2)}, u32[]{:S(2)}) collective-permute-start(f32[18,1,512]{2,1,0:T(1,128)S(1)} %get-tuple-element.11), channel_id=1, source_target_pairs={{1,0},{2,1},{3,2},{4,3},{5,4},{6,5},{7,6},{9,8},{10,9},{11,10},{12... | collective-permute-start | bytes 110600 | tf_op jit(solution)/shard_map/ppermute | solution.py:18
  116.7 5.0 %collective-permute-start.18 = (f32[1,8,512]{2,1,0:T(8,128)S(1)}, f32[1,8,512]{2,1,0:T(8,128)S(1)}, u32[]{:S(2)}, u32[]{:S(2)}) collective-permute-start(f32[1,8,512]{2,1,0:T(8,128)S(1)} %get-tuple-element.20), channel_id=1, source_target_pairs={{0,8},{8,16},{16,24},{1,9},{9,17},{17,25},{2,10},{10,18},{18,26},{... | collective-permute-start | bytes 49160 | tf_op jit(solution)/shard_map/ppermute | solution.py:15
  119.5 5.6 %collective-permute-start.19 = (f32[1,8,512]{2,1,0:T(8,128)S(1)}, f32[1,8,512]{2,1,0:T(8,128)S(1)}, u32[]{:S(2)}, u32[]{:S(2)}) collective-permute-start(f32[1,8,512]{2,1,0:T(8,128)S(1)} %get-tuple-element.21), channel_id=1, source_target_pairs={{8,0},{16,8},{24,16},{9,1},{17,9},{25,17},{10,2},{18,10},{26,18},{... | collective-permute-start | bytes 49160 | tf_op jit(solution)/shard_map/ppermute | solution.py:18
  125.2 4.9 %collective-permute-start.20 = (f32[18,1,512]{2,1,0:T(1,128)S(1)}, f32[18,1,512]{2,1,0:T(1,128)S(1)}, u32[]{:S(2)}, u32[]{:S(2)}) collective-permute-start(f32[18,1,512]{2,1,0:T(1,128)S(1)} %get-tuple-element.8), channel_id=1, source_target_pairs={{0,1},{1,2},{2,3},{3,4},{4,5},{5,6},{6,7},{8,9},{9,10},{10,11},{11... | collective-permute-start | bytes 110600 | tf_op jit(solution)/shard_map/ppermute | solution.py:15
  128.4 4.0 %collective-permute-start.21 = (f32[18,1,512]{2,1,0:T(1,128)S(1)}, f32[18,1,512]{2,1,0:T(1,128)S(1)}, u32[]{:S(2)}, u32[]{:S(2)}) collective-permute-start(f32[18,1,512]{2,1,0:T(1,128)S(1)} %get-tuple-element.9), channel_id=1, source_target_pairs={{1,0},{2,1},{3,2},{4,3},{5,4},{6,5},{7,6},{9,8},{10,9},{11,10},{12... | collective-permute-start | bytes 110600 | tf_op jit(solution)/shard_map/ppermute | solution.py:18
where the time goes:
time: 222 us; the launch traced here: 220 us
  blocking collectives  84.9 us (38%)
  starting transfers between devices  46.7 us (21%)
  between operations  34.1 us (15%)
  waiting for transfers between devices  31.1 us (14%)
  local copies, waits for them, and re-layouts  12.5 us (6%)
  matrix products  6.41 us (3%)
  other arithmetic  4.38 us (2%)
    psum x1, blocking collectives, local(): squares = lax.psum(jnp.sum(residual0 * residual0), ('gx', 'gy'))  44 us
    psum x1, blocking collectives, local(): gram = lax.psum(local_gram, ('gx', 'gy')) / cells  40.9 us
    ppermute x10, starting transfers between devices, padded(): lax.ppermute(lax.slice_in_dim(block, block.shape[dim] - width, None, axis...  31.2 us
    ppermute x10, waiting for transfers between devices, padded(): lax.ppermute(lax.slice_in_dim(block, 0, width, axis=dim), axis, backward)  30.7 us
    ppermute x10, starting transfers between devices, padded(): lax.ppermute(lax.slice_in_dim(block, 0, width, axis=dim), axis, backward)  12.9 us
    dot_general x1, matrix products, local(): jnp.einsum('axyz,bxyz->ab', block, block, precision=lax.Precision.HIGHEST)  4.56 us
  transfers between devices with their start and end apart: 22, of which 13 were waited for; matrix products, arithmetic and copies ran while one was open for 3% of the time, Pallas kernels for 0%

commit v1 on v0

--- a/solution.py
+++ b/solution.py
@@ -1,10 +1,19 @@
+import functools
 import jax
 import jax.numpy as jnp
 from jax import lax
 from jax.sharding import PartitionSpec as P
+from jax.lax import psum
 
 STEPS = 4
 EPS = 1e-06
+
+
+def carry_paths(v0, mesh_name, mesh_dim):
+    return psum(psum(v0, mesh_name), mesh_dim)
+
+
+change_stages_all = functools.partial(carry_paths, mesh_name="gy", mesh_dim="gx")
 
 
 def padded(block, sides, width):
@@ -95,7 +104,7 @@
         basis.append(vector)
     block = jnp.stack(basis)
     local_gram = jnp.einsum("axyz,bxyz->ab", block, block, precision=lax.Precision.HIGHEST)
-    gram = lax.psum(local_gram, ("gx", "gy")) / cells
+    gram = change_stages_all(local_gram) / cells
     upper = jnp.linalg.cholesky(gram).T
     inverse = upper_inverse(upper)
     ortho = jnp.einsum("jk,jxyz->kxyz", inverse, block, precision=lax.Precision.HIGHEST)

time: 222 us -> 205 us (0.923)
  blocking collectives: 84.9 us -> 68.7 us
    psum x1 -> x2, blocking collectives: 40.9 us -> 24.6 us  [carry_paths(): return psum(psum(v0, mesh_name), mesh_dim)]
where the time goes in v1:
time: 205 us; the launch traced here: 204 us
  blocking collectives  68.7 us (34%)
  starting transfers between devices  46.7 us (23%)
  between operations  34 us (17%)
  waiting for transfers between devices  31.1 us (15%)
  local copies, waits for them, and re-layouts  12.5 us (6%)
  matrix products  6.41 us (3%)
  other arithmetic  4.39 us (2%)
    psum x1, blocking collectives, local(): squares = lax.psum(jnp.sum(residual0 * residual0), ('gx', 'gy'))  44 us
    ppermute x10, starting transfers between devices, padded(): lax.ppermute(lax.slice_in_dim(block, block.shape[dim] - width, None, axis...  31.2 us
    ppermute x10, waiting for transfers between devices, padded(): lax.ppermute(lax.slice_in_dim(block, 0, width, axis=dim), axis, backward)  30.7 us
    psum x2, blocking collectives, carry_paths(): return psum(psum(v0, mesh_name), mesh_dim)  24.6 us
    ppermute x10, starting transfers between devices, padded(): lax.ppermute(lax.slice_in_dim(block, 0, width, axis=dim), axis, backward)  12.9 us
    dot_general x1, matrix products, local(): jnp.einsum('axyz,bxyz->ab', block, block, precision=lax.Precision.HIGHEST)  4.56 us
  transfers between devices with their start and end apart: 22, of which 13 were waited for; matrix products, arithmetic and copies ran while one was open for 3% of the time, Pallas kernels for 0%

profile of v1, /device:TPU:0, one launch (start us, length us, event | category | flops | bytes accessed | tf_op | source)
XLA Modules:
  0.0 203.7 jit_solution(2842288891122812743)
XLA Ops:
  0.7 0.8 fusion.73
  1.5 4.8 %collective-permute-start.2 = (f32[1,8,512]{2,1,0:T(8,128)S(1)}, f32[1,8,512]{2,1,0:T(8,128)S(1)}, u32[]{:S(2)}, u32[]{:S(2)}) collective-permute-start(f32[1,8,512]{2,1,0:T(8,128)S(1)} %get-tuple-element.35), channel_id=1, source_target_pairs={{0,8},{8,16},{16,24},{1,9},{9,17},{17,25},{2,10},{10,18},{18,26},{... | collective-permute-start | bytes 49160 | tf_op jit(solution)/shard_map/ppermute | solution.py:24
  6.4 0.7 slice.332
  7.1 1.3 collective-permute-start
  8.4 1.3 collective-permute-start.3
  9.7 1.0 slice.334
  10.7 1.3 collective-permute-start.1
  12.0 1.0 constant_dynamic-update-slice_fusion.1
  13.0 1.7 collective-permute-done.3
  14.7 1.4 collective-permute-start.4
  16.1 1.3 collective-permute-start.5
  17.4 1.2 fusion.74
  18.6 0.1 slice.336
  18.7 2.2 %collective-permute-done.5 = f32[18,1,512]{2,1,0:T(1,128)S(1)} collective-permute-done((f32[18,1,512]{2,1,0:T(1,128)S(1)}, f32[18,1,512]{2,1,0:T(1,128)S(1)}, u32[]{:S(2)}, u32[]{:S(2)}) %collective-permute-start.5) | collective-permute-done | bytes 36896 | tf_op jit(solution)/shard_map/ppermute | solution.py:27
  21.0 1.0 multiply_reduce_fusion
  21.9 44.0 %psum.21 = f32[]{:T(128)} all-reduce(f32[]{:T(128)} %get-tuple-element.6), channel_id=1, replica_groups=mesh['gx'=4,'gy'=8] {'gx','gy'}, use_global_device_ids=true, to_apply=%region_1.2 | all-reduce | flops 1 | bytes 8 | tf_op jit(solution)/shard_map/psum | solution.py:97
  66.7 4.2 %collective-permute-start.6 = (f32[1,8,512]{2,1,0:T(8,128)S(1)}, f32[1,8,512]{2,1,0:T(8,128)S(1)}, u32[]{:S(2)}, u32[]{:S(2)}) collective-permute-start(f32[1,8,512]{2,1,0:T(8,128)S(1)} %get-tuple-element.32), channel_id=1, source_target_pairs={{0,8},{8,16},{16,24},{1,9},{9,17},{17,25},{2,10},{10,18},{18,26},{... | collective-permute-start | bytes 49160 | tf_op jit(solution)/shard_map/ppermute | solution.py:24
  70.9 1.3 collective-permute-start.7
  72.3 4.2 %collective-permute-done.7 = f32[1,8,512]{2,1,0:T(8,128)S(1)} collective-permute-done((f32[1,8,512]{2,1,0:T(8,128)S(1)}, f32[1,8,512]{2,1,0:T(8,128)S(1)}, u32[]{:S(2)}, u32[]{:S(2)}) %collective-permute-start.7) | collective-permute-done | bytes 16416 | tf_op jit(solution)/shard_map/ppermute | solution.py:27
  76.6 1.3 collective-permute-start.8
  77.9 1.3 collective-permute-start.9
  79.2 0.1 fusion.71
  79.3 3.2 %collective-permute-done.9 = f32[18,1,512]{2,1,0:T(1,128)S(1)} collective-permute-done((f32[18,1,512]{2,1,0:T(1,128)S(1)}, f32[18,1,512]{2,1,0:T(1,128)S(1)}, u32[]{:S(2)}, u32[]{:S(2)}) %collective-permute-start.9) | collective-permute-done | bytes 36896 | tf_op jit(solution)/shard_map/ppermute | solution.py:27
  82.6 0.3 fusion.38
  82.9 4.5 %collective-permute-start.10 = (f32[1,8,512]{2,1,0:T(8,128)S(1)}, f32[1,8,512]{2,1,0:T(8,128)S(1)}, u32[]{:S(2)}, u32[]{:S(2)}) collective-permute-start(f32[1,8,512]{2,1,0:T(8,128)S(1)} %get-tuple-element.28), channel_id=1, source_target_pairs={{0,8},{8,16},{16,24},{1,9},{9,17},{17,25},{2,10},{10,18},{18,26},{... | collective-permute-start | bytes 49160 | tf_op jit(solution)/shard_map/ppermute | solution.py:24
  87.4 1.3 collective-permute-start.11
  88.8 4.2 %collective-permute-done.11 = f32[1,8,512]{2,1,0:T(8,128)S(1)} collective-permute-done((f32[1,8,512]{2,1,0:T(8,128)S(1)}, f32[1,8,512]{2,1,0:T(8,128)S(1)}, u32[]{:S(2)}, u32[]{:S(2)}) %collective-permute-start.11) | collective-permute-done | bytes 16416 | tf_op jit(solution)/shard_map/ppermute | solution.py:27
  93.1 3.1 %collective-permute-start.12 = (f32[18,1,512]{2,1,0:T(1,128)S(1)}, f32[18,1,512]{2,1,0:T(1,128)S(1)}, u32[]{:S(2)}, u32[]{:S(2)}) collective-permute-start(f32[18,1,512]{2,1,0:T(1,128)S(1)} %get-tuple-element.12), channel_id=1, source_target_pairs={{0,1},{1,2},{2,3},{3,4},{4,5},{5,6},{6,7},{8,9},{9,10},{10,11},{11... | collective-permute-start | bytes 110600 | tf_op jit(solution)/shard_map/ppermute | solution.py:24
  96.2 1.3 collective-permute-start.13
  97.5 0.1 fusion.69
  97.7 2.6 %collective-permute-done.13 = f32[18,1,512]{2,1,0:T(1,128)S(1)} collective-permute-done((f32[18,1,512]{2,1,0:T(1,128)S(1)}, f32[18,1,512]{2,1,0:T(1,128)S(1)}, u32[]{:S(2)}, u32[]{:S(2)}) %collective-permute-start.13) | collective-permute-done | bytes 36896 | tf_op jit(solution)/shard_map/ppermute | solution.py:27
  100.3 0.3 fusion.27
  100.6 2.8 %collective-permute-start.14 = (f32[1,8,512]{2,1,0:T(8,128)S(1)}, f32[1,8,512]{2,1,0:T(8,128)S(1)}, u32[]{:S(2)}, u32[]{:S(2)}) collective-permute-start(f32[1,8,512]{2,1,0:T(8,128)S(1)} %get-tuple-element.24), channel_id=1, source_target_pairs={{0,8},{8,16},{16,24},{1,9},{9,17},{17,25},{2,10},{10,18},{18,26},{... | collective-permute-start | bytes 49160 | tf_op jit(solution)/shard_map/ppermute | solution.py:24
  103.5 1.3 collective-permute-start.15
  104.9 4.2 %collective-permute-done.15 = f32[1,8,512]{2,1,0:T(8,128)S(1)} collective-permute-done((f32[1,8,512]{2,1,0:T(8,128)S(1)}, f32[1,8,512]{2,1,0:T(8,128)S(1)}, u32[]{:S(2)}, u32[]{:S(2)}) %collective-permute-start.15) | collective-permute-done | bytes 16416 | tf_op jit(solution)/shard_map/ppermute | solution.py:27
  109.1 3.1 %collective-permute-start.16 = (f32[18,1,512]{2,1,0:T(1,128)S(1)}, f32[18,1,512]{2,1,0:T(1,128)S(1)}, u32[]{:S(2)}, u32[]{:S(2)}) collective-permute-start(f32[18,1,512]{2,1,0:T(1,128)S(1)} %get-tuple-element.10), channel_id=1, source_target_pairs={{0,1},{1,2},{2,3},{3,4},{4,5},{5,6},{6,7},{8,9},{9,10},{10,11},{11... | collective-permute-start | bytes 110600 | tf_op jit(solution)/shard_map/ppermute | solution.py:24
  112.3 1.3 collective-permute-start.17
  113.6 0.1 fusion.67
  113.7 2.6 %collective-permute-done.17 = f32[18,1,512]{2,1,0:T(1,128)S(1)} collective-permute-done((f32[18,1,512]{2,1,0:T(1,128)S(1)}, f32[18,1,512]{2,1,0:T(1,128)S(1)}, u32[]{:S(2)}, u32[]{:S(2)}) %collective-permute-start.17) | collective-permute-done | bytes 36896 | tf_op jit(solution)/shard_map/ppermute | solution.py:27
  116.3 0.3 fusion.16
  116.7 2.8 %collective-permute-start.18 = (f32[1,8,512]{2,1,0:T(8,128)S(1)}, f32[1,8,512]{2,1,0:T(8,128)S(1)}, u32[]{:S(2)}, u32[]{:S(2)}) collective-permute-start(f32[1,8,512]{2,1,0:T(8,128)S(1)} %get-tuple-element.20), channel_id=1, source_target_pairs={{0,8},{8,16},{16,24},{1,9},{9,17},{17,25},{2,10},{10,18},{18,26},{... | collective-permute-start | bytes 49160 | tf_op jit(solution)/shard_map/ppermute | solution.py:24
  119.5 1.3 collective-permute-start.19
  120.9 0.3 copy.9
  121.1 0.3 copy.10
  121.4 0.3 copy.11
  121.7 3.5 %collective-permute-done.19 = f32[1,8,512]{2,1,0:T(8,128)S(1)} collective-permute-done((f32[1,8,512]{2,1,0:T(8,128)S(1)}, f32[1,8,512]{2,1,0:T(8,128)S(1)}, u32[]{:S(2)}, u32[]{:S(2)}) %collective-permute-start.19) | collective-permute-done | bytes 16416 | tf_op jit(solution)/shard_map/ppermute | solution.py:27
  125.2 3.1 %collective-permute-start.20 = (f32[18,1,512]{2,1,0:T(1,128)S(1)}, f32[18,1,512]{2,1,0:T(1,128)S(1)}, u32[]{:S(2)}, u32[]{:S(2)}) collective-permute-start(f32[18,1,512]{2,1,0:T(1,128)S(1)} %get-tuple-element.8), channel_id=1, source_target_pairs={{0,1},{1,2},{2,3},{3,4},{4,5},{5,6},{6,7},{8,9},{9,10},{10,11},{11... | collective-permute-start | bytes 110600 | tf_op jit(solution)/shard_map/ppermute | solution.py:24
  128.4 1.3 collective-permute-start.21
  129.7 0.1 fusion.65
  129.8 0.3 copy.12
  130.1 2.3 %collective-permute-done.21 = f32[18,1,512]{2,1,0:T(1,128)S(1)} collective-permute-done((f32[18,1,512]{2,1,0:T(1,128)S(1)}, f32[18,1,512]{2,1,0:T(1,128)S(1)}, u32[]{:S(2)}, u32[]{:S(2)}) %collective-permute-start.21) | collective-permute-done | bytes 36896 | tf_op jit(solution)/shard_map/ppermute | solution.py:27
  132.4 0.4 fusion.5
  132.8 0.2 stack.118
  132.9 2.1 %stack.119 = f32[5,16,8,512]{3,0,2,1:T(8,128)S(1)} concatenate(f32[1,16,8,512]{3,0,2,1:T(1,128)S(1)} %copy.9, f32[1,16,8,512]{3,0,2,1:T(1,128)S(1)} %copy.10, f32[1,16,8,512]{3,0,2,1:T(1,128)S(1)} %copy.11, f32[1,16,8,512]{3,0,2,1:T(1,128)S(1)} %copy.12, f32[1,16,8,512]{3,0,2,1:T(1,128)S(1)} %stack.118), dimensions={0} | concatenate | bytes 2621440 | tf_op jit(solution)/shard_map/stack | solution.py:105
  135.0 4.6 %convolution_bitcast_fusion = f32[5,5]{0,1:T(8,128)S(1)} fusion(f32[5,16,8,512]{3,0,2,1:T(8,128)S(1)} %stack.119), kind=kOutput, calls=%fused_computation | convolution fusion | flops 19660800 | bytes 1310820 | tf_op jit(solution)/shard_map/axyz,bxyz->ab/dot_general | solution.py:106
  139.6 16.3 %psum.22 = f32[5,5]{0,1:T(8,128)S(1)} all-reduce(f32[5,5]{0,1:T(8,128)S(1)} %convolution_bitcast_fusion), channel_id=1, replica_groups=mesh['gx'=4,'gy'=8] {'gy'}, use_global_device_ids=true, to_apply=%region_2.3 | all-reduce | flops 25 | bytes 200 | tf_op jit(solution)/shard_map/psum | solution.py:13
  155.8 8.4 %psum.23 = f32[5,5]{0,1:T(8,128)S(1)} all-reduce(f32[5,5]{0,1:T(8,128)S(1)} %psum.22), channel_id=1, replica_groups=mesh['gx'=4,'gy'=8] {'gx'}, use_global_device_ids=true, to_apply=%region_3.4 | all-reduce | flops 25 | bytes 200 | tf_op jit(solution)/shard_map/psum | solution.py:13
  164.3 0.4 cholesky.18
  164.8 0.6 compare_reduce_fusion
  165.5 0.6 select_bitcast_fusion
  166.1 0.7 copy.16
  166.8 0.7 fusion.75
  198.9 1.8 fusion.60
  200.7 1.8 copy.15
  (47 shorter events, 1.3 us)
Async XLA Ops:
  0.6 20.3 %copy-start.4 = (f32[16,8,512]{2,1,0:T(8,128)S(1)}, f32[16,8,512]{2,1,0:T(8,128)}, u32[]{:S(2)}) copy-start(f32[16,8,512]{2,1,0:T(8,128)} %param.6) | copy-start | bytes 786436
  0.6 20.3 %copy-start.2 = (f32[16,8,512]{2,1,0:T(8,128)S(1)}, f32[16,8,512]{2,1,0:T(8,128)}, u32[]{:S(2)}) copy-start(f32[16,8,512]{2,1,0:T(8,128)} %param.9) | copy-start | bytes 786436
  0.7 20.3 %copy-start.1 = (f32[16,8,512]{2,1,0:T(8,128)S(1)}, f32[16,8,512]{2,1,0:T(8,128)}, u32[]{:S(2)}) copy-start(f32[16,8,512]{2,1,0:T(8,128)} %param.10) | copy-start | bytes 786436
  0.7 17.9 %copy-start = (f32[16,8,512]{2,1,0:T(8,128)S(1)}, f32[16,8,512]{2,1,0:T(8,128)}, u32[]{:S(2)}) copy-start(f32[16,8,512]{2,1,0:T(8,128)} %param.11) | copy-start | bytes 786436
  0.7 20.3 %copy-start.3 = (f32[16,8,512]{2,1,0:T(8,128)S(1)}, f32[16,8,512]{2,1,0:T(8,128)}, u32[]{:S(2)}) copy-start(f32[16,8,512]{2,1,0:T(8,128)} %param.8) | copy-start | bytes 786436
  0.7 20.3 %copy-start.5 = (f32[16,8,512]{2,1,0:T(8,128)S(1)}, f32[16,8,512]{2,1,0:T(8,128)}, u32[]{:S(2)}) copy-start(f32[16,8,512]{2,1,0:T(8,128)} %param.7) | copy-start | bytes 786436
  1.5 10.4 %collective-permute-start.2 = (f32[1,8,512]{2,1,0:T(8,128)S(1)}, f32[1,8,512]{2,1,0:T(8,128)S(1)}, u32[]{:S(2)}, u32[]{:S(2)}) collective-permute-start(f32[1,8,512]{2,1,0:T(8,128)S(1)} %get-tuple-element.35), channel_id=1, source_target_pairs={{0,8},{8,16},{16,24},{1,9},{9,17},{17,25},{2,10},{10,18},{18,26},{... | collective-permute-start | bytes 49160 | tf_op jit(solution)/shard_map/ppermute | solution.py:24
  7.1 11.6 %collective-permute-start = (f32[1,8,512]{2,1,0:T(8,128)S(1)}, f32[1,8,512]{2,1,0:T(8,128)S(1)}, u32[]{:S(2)}, u32[]{:S(2)}) collective-permute-start(f32[1,8,512]{2,1,0:T(8,128)S(1)} %slice.332), channel_id=1, source_target_pairs={{8,0},{16,8},{24,16},{9,1},{17,9},{25,17},{10,2},{18,10},{26,18},{... | collective-permute-start | bytes 49160 | tf_op jit(solution)/shard_map/ppermute | solution.py:35
  8.4 6.3 %collective-permute-start.3 = (f32[1,8,512]{2,1,0:T(8,128)S(1)}, f32[1,8,512]{2,1,0:T(8,128)S(1)}, u32[]{:S(2)}, u32[]{:S(2)}) collective-permute-start(f32[1,8,512]{2,1,0:T(8,128)S(1)} %get-tuple-element.34), channel_id=1, source_target_pairs={{8,0},{16,8},{24,16},{9,1},{17,9},{25,17},{10,2},{18,10},{26,18},{... | collective-permute-start | bytes 49160 | tf_op jit(solution)/shard_map/ppermute | solution.py:27
  10.7 8.0 %collective-permute-start.1 = (f32[16,1,512]{2,1,0:T(1,128)S(1)}, f32[16,1,512]{2,1,0:T(1,128)S(1)}, u32[]{:S(2)}, u32[]{:S(2)}) collective-permute-start(f32[16,1,512]{2,1,0:T(1,128)S(1)} %slice.334), channel_id=1, source_target_pairs={{1,0},{2,1},{3,2},{4,3},{5,4},{6,5},{7,6},{9,8},{10,9},{11,10},{12... | collective-permute-start | bytes 98312 | tf_op jit(solution)/shard_map/ppermute | solution.py:35
  14.7 4.0 %collective-permute-start.4 = (f32[18,1,512]{2,1,0:T(1,128)S(1)}, f32[18,1,512]{2,1,0:T(1,128)S(1)}, u32[]{:S(2)}, u32[]{:S(2)}) collective-permute-start(f32[18,1,512]{2,1,0:T(1,128)S(1)} %get-tuple-element.16), channel_id=1, source_target_pairs={{0,1},{1,2},{2,3},{3,4},{4,5},{5,6},{6,7},{8,9},{9,10},{10,11},{11... | collective-permute-start | bytes 110600 | tf_op jit(solution)/shard_map/ppermute | solution.py:24
  16.1 4.8 %collective-permute-start.5 = (f32[18,1,512]{2,1,0:T(1,128)S(1)}, f32[18,1,512]{2,1,0:T(1,128)S(1)}, u32[]{:S(2)}, u32[]{:S(2)}) collective-permute-start(f32[18,1,512]{2,1,0:T(1,128)S(1)} %get-tuple-element.17), channel_id=1, source_target_pairs={{1,0},{2,1},{3,2},{4,3},{5,4},{6,5},{7,6},{9,8},{10,9},{11,10},{12... | collective-permute-start | bytes 110600 | tf_op jit(solution)/shard_map/ppermute | solution.py:27
  66.7 5.6 %collective-permute-start.6 = (f32[1,8,512]{2,1,0:T(8,128)S(1)}, f32[1,8,512]{2,1,0:T(8,128)S(1)}, u32[]{:S(2)}, u32[]{:S(2)}) collective-permute-start(f32[1,8,512]{2,1,0:T(8,128)S(1)} %get-tuple-element.32), channel_id=1, source_target_pairs={{0,8},{8,16},{16,24},{1,9},{9,17},{17,25},{2,10},{10,18},{18,26},{... | collective-permute-start | bytes 49160 | tf_op jit(solution)/shard_map/ppermute | solution.py:24
  70.9 5.6 %collective-permute-start.7 = (f32[1,8,512]{2,1,0:T(8,128)S(1)}, f32[1,8,512]{2,1,0:T(8,128)S(1)}, u32[]{:S(2)}, u32[]{:S(2)}) collective-permute-start(f32[1,8,512]{2,1,0:T(8,128)S(1)} %get-tuple-element.33), channel_id=1, source_target_pairs={{8,0},{16,8},{24,16},{9,1},{17,9},{25,17},{10,2},{18,10},{26,18},{... | collective-permute-start | bytes 49160 | tf_op jit(solution)/shard_map/ppermute | solution.py:27
  76.6 2.7 %collective-permute-start.8 = (f32[18,1,512]{2,1,0:T(1,128)S(1)}, f32[18,1,512]{2,1,0:T(1,128)S(1)}, u32[]{:S(2)}, u32[]{:S(2)}) collective-permute-start(f32[18,1,512]{2,1,0:T(1,128)S(1)} %get-tuple-element.14), channel_id=1, source_target_pairs={{0,1},{1,2},{2,3},{3,4},{4,5},{5,6},{6,7},{8,9},{9,10},{10,11},{11... | collective-permute-start | bytes 110600 | tf_op jit(solution)/shard_map/ppermute | solution.py:24
  77.9 4.7 %collective-permute-start.9 = (f32[18,1,512]{2,1,0:T(1,128)S(1)}, f32[18,1,512]{2,1,0:T(1,128)S(1)}, u32[]{:S(2)}, u32[]{:S(2)}) collective-permute-start(f32[18,1,512]{2,1,0:T(1,128)S(1)} %get-tuple-element.15), channel_id=1, source_target_pairs={{1,0},{2,1},{3,2},{4,3},{5,4},{6,5},{7,6},{9,8},{10,9},{11,10},{12... | collective-permute-start | bytes 110600 | tf_op jit(solution)/shard_map/ppermute | solution.py:27
  82.9 5.9 %collective-permute-start.10 = (f32[1,8,512]{2,1,0:T(8,128)S(1)}, f32[1,8,512]{2,1,0:T(8,128)S(1)}, u32[]{:S(2)}, u32[]{:S(2)}) collective-permute-start(f32[1,8,512]{2,1,0:T(8,128)S(1)} %get-tuple-element.28), channel_id=1, source_target_pairs={{0,8},{8,16},{16,24},{1,9},{9,17},{17,25},{2,10},{10,18},{18,26},{... | collective-permute-start | bytes 49160 | tf_op jit(solution)/shard_map/ppermute | solution.py:24
  87.4 5.6 %collective-permute-start.11 = (f32[1,8,512]{2,1,0:T(8,128)S(1)}, f32[1,8,512]{2,1,0:T(8,128)S(1)}, u32[]{:S(2)}, u32[]{:S(2)}) collective-permute-start(f32[1,8,512]{2,1,0:T(8,128)S(1)} %get-tuple-element.29), channel_id=1, source_target_pairs={{8,0},{16,8},{24,16},{9,1},{17,9},{25,17},{10,2},{18,10},{26,18},{... | collective-permute-start | bytes 49160 | tf_op jit(solution)/shard_map/ppermute | solution.py:27
  93.1 4.6 %collective-permute-start.12 = (f32[18,1,512]{2,1,0:T(1,128)S(1)}, f32[18,1,512]{2,1,0:T(1,128)S(1)}, u32[]{:S(2)}, u32[]{:S(2)}) collective-permute-start(f32[18,1,512]{2,1,0:T(1,128)S(1)} %get-tuple-element.12), channel_id=1, source_target_pairs={{0,1},{1,2},{2,3},{3,4},{4,5},{5,6},{6,7},{8,9},{9,10},{10,11},{11... | collective-permute-start | bytes 110600 | tf_op jit(solution)/shard_map/ppermute | solution.py:24
  96.2 4.0 %collective-permute-start.13 = (f32[18,1,512]{2,1,0:T(1,128)S(1)}, f32[18,1,512]{2,1,0:T(1,128)S(1)}, u32[]{:S(2)}, u32[]{:S(2)}) collective-permute-start(f32[18,1,512]{2,1,0:T(1,128)S(1)} %get-tuple-element.13), channel_id=1, source_target_pairs={{1,0},{2,1},{3,2},{4,3},{5,4},{6,5},{7,6},{9,8},{10,9},{11,10},{12... | collective-permute-start | bytes 110600 | tf_op jit(solution)/shard_map/ppermute | solution.py:27
  100.6 4.3 %collective-permute-start.14 = (f32[1,8,512]{2,1,0:T(8,128)S(1)}, f32[1,8,512]{2,1,0:T(8,128)S(1)}, u32[]{:S(2)}, u32[]{:S(2)}) collective-permute-start(f32[1,8,512]{2,1,0:T(8,128)S(1)} %get-tuple-element.24), channel_id=1, source_target_pairs={{0,8},{8,16},{16,24},{1,9},{9,17},{17,25},{2,10},{10,18},{18,26},{... | collective-permute-start | bytes 49160 | tf_op jit(solution)/shard_map/ppermute | solution.py:24
  103.5 5.6 %collective-permute-start.15 = (f32[1,8,512]{2,1,0:T(8,128)S(1)}, f32[1,8,512]{2,1,0:T(8,128)S(1)}, u32[]{:S(2)}, u32[]{:S(2)}) collective-permute-start(f32[1,8,512]{2,1,0:T(8,128)S(1)} %get-tuple-element.25), channel_id=1, source_target_pairs={{8,0},{16,8},{24,16},{9,1},{17,9},{25,17},{10,2},{18,10},{26,18},{... | collective-permute-start | bytes 49160 | tf_op jit(solution)/shard_map/ppermute | solution.py:27
  109.1 4.6 %collective-permute-start.16 = (f32[18,1,512]{2,1,0:T(1,128)S(1)}, f32[18,1,512]{2,1,0:T(1,128)S(1)}, u32[]{:S(2)}, u32[]{:S(2)}) collective-permute-start(f32[18,1,512]{2,1,0:T(1,128)S(1)} %get-tuple-element.10), channel_id=1, source_target_pairs={{0,1},{1,2},{2,3},{3,4},{4,5},{5,6},{6,7},{8,9},{9,10},{10,11},{11... | collective-permute-start | bytes 110600 | tf_op jit(solution)/shard_map/ppermute | solution.py:24
  112.3 4.0 %collective-permute-start.17 = (f32[18,1,512]{2,1,0:T(1,128)S(1)}, f32[18,1,512]{2,1,0:T(1,128)S(1)}, u32[]{:S(2)}, u32[]{:S(2)}) collective-permute-start(f32[18,1,512]{2,1,0:T(1,128)S(1)} %get-tuple-element.11), channel_id=1, source_target_pairs={{1,0},{2,1},{3,2},{4,3},{5,4},{6,5},{7,6},{9,8},{10,9},{11,10},{12... | collective-permute-start | bytes 110600 | tf_op jit(solution)/shard_map/ppermute | solution.py:27
  116.7 5.0 %collective-permute-start.18 = (f32[1,8,512]{2,1,0:T(8,128)S(1)}, f32[1,8,512]{2,1,0:T(8,128)S(1)}, u32[]{:S(2)}, u32[]{:S(2)}) collective-permute-start(f32[1,8,512]{2,1,0:T(8,128)S(1)} %get-tuple-element.20), channel_id=1, source_target_pairs={{0,8},{8,16},{16,24},{1,9},{9,17},{17,25},{2,10},{10,18},{18,26},{... | collective-permute-start | bytes 49160 | tf_op jit(solution)/shard_map/ppermute | solution.py:24
  119.5 5.6 %collective-permute-start.19 = (f32[1,8,512]{2,1,0:T(8,128)S(1)}, f32[1,8,512]{2,1,0:T(8,128)S(1)}, u32[]{:S(2)}, u32[]{:S(2)}) collective-permute-start(f32[1,8,512]{2,1,0:T(8,128)S(1)} %get-tuple-element.21), channel_id=1, source_target_pairs={{8,0},{16,8},{24,16},{9,1},{17,9},{25,17},{10,2},{18,10},{26,18},{... | collective-permute-start | bytes 49160 | tf_op jit(solution)/shard_map/ppermute | solution.py:27
  125.2 4.9 %collective-permute-start.20 = (f32[18,1,512]{2,1,0:T(1,128)S(1)}, f32[18,1,512]{2,1,0:T(1,128)S(1)}, u32[]{:S(2)}, u32[]{:S(2)}) collective-permute-start(f32[18,1,512]{2,1,0:T(1,128)S(1)} %get-tuple-element.8), channel_id=1, source_target_pairs={{0,1},{1,2},{2,3},{3,4},{4,5},{5,6},{6,7},{8,9},{9,10},{10,11},{11... | collective-permute-start | bytes 110600 | tf_op jit(solution)/shard_map/ppermute | solution.py:24
  128.4 4.0 %collective-permute-start.21 = (f32[18,1,512]{2,1,0:T(1,128)S(1)}, f32[18,1,512]{2,1,0:T(1,128)S(1)}, u32[]{:S(2)}, u32[]{:S(2)}) collective-permute-start(f32[18,1,512]{2,1,0:T(1,128)S(1)} %get-tuple-element.9), channel_id=1, source_target_pairs={{1,0},{2,1},{3,2},{4,3},{5,4},{6,5},{7,6},{9,8},{10,9},{11,10},{12... | collective-permute-start | bytes 110600 | tf_op jit(solution)/shard_map/ppermute | solution.py:27
